TPU v7x, 512 devices: a whole 4x8x8 slice. The times are simulated.
512 devices in a mesh: space: 64 (over x, y_hi, z), chan: 8 (over y_lo, core).
Axes of the slice: x: 4, y: 8 (y_hi: 2, y_lo: 4; y = y_hi * 4 + y_lo), z: 8, core: 2. Of those that a mesh axis runs over, the one named last changes fastest.
Arguments:
- activation: float32 [64, 2, 512, 256], P('space', None, 'chan'), may hold values from -6 to 6
- weight: bfloat16 [3, 3, 3, 512, 512], P(None, None, None, 'chan'), may hold values from -0.0546875 to 0.0546875
- conv_bias: float32 [512], P('chan'), may hold values from -3 to 3
Outputs:
- output: float32 [64, 2, 512, 256], P('space', None, 'chan')
All inputs are finite; a program needn't handle non-finite values.
Results may differ from a plain program's by a relative error of at most 0.0026.
Values may be sent and summed in bfloat16 or wider, within the bound.
No kernel may reach another device: no remote copies, remote signals or barrier semaphores. Data moves between devices by JAX's collectives and lax.ppermute only.
A program may use at most 64 MiB of HBM per device.

v0:
```python
import jax
import jax.numpy as jnp
from jax import lax
from jax.sharding import PartitionSpec as P

CY = 8
negative_slope = 0.3


def cross(lower_source, upper_source, axis, steps):
    count = lax.axis_size(axis)
    width = lax.axis_size("chan")
    run_y = width // 2
    pairs = []
    for source in range(count):
        for lane in range(width):
            place, core = divmod(lane, 2)
            target = (source + (steps if core == 0 else -steps)) % count
            crosses = source // CY % 2 != target // CY % 2
            moved = (place + run_y // 2) % run_y * 2 + core if crosses else lane
            pairs.append((source * width + lane, target * width + moved))
    on_first = lax.axis_index("chan") % 2 == 0
    sent = jnp.where(on_first, lower_source, upper_source)
    return lax.ppermute(sent, (axis, "chan"), pairs)


def swap(got):
    width = lax.axis_size("chan")
    on_first = lax.axis_index("chan") % 2 == 0
    swapped = lax.ppermute(got, "chan", [(lane, lane ^ 1) for lane in range(width)])
    return (jnp.where(on_first, got, swapped), jnp.where(on_first, swapped, got))


def conv(field, taps, padding):
    return lax.conv_general_dilated(
        field[None],
        taps,
        window_strides=(1, 1, 1),
        padding=padding,
        dimension_numbers=("NCDHW", "DHWOI", "NDCHW"),
        preferred_element_type=jnp.float32,
    )[0]


def body(activation, weight, conv_bias):
    size_x = activation.shape[1]
    size_y = CY
    size_z = activation.shape[3] // size_y
    own_block = activation[0].astype(jnp.bfloat16).transpose(1, 0, 2)
    gathered = lax.all_gather(own_block, "chan", axis=0, tiled=True)
    gathered = gathered.reshape(-1, size_x, size_y, size_z)
    own_part = conv(gathered, weight, ((1, 1), (1, 1), (1, 1)))
    width_in = gathered.shape[0]
    got = [
        cross(gathered[:, -1:], gathered[:, :1], "space", CY),
        cross(gathered[:, :, -1:], gathered[:, :, :1], "space", 1),
    ]
    corners_from, own_part = lax.optimization_barrier(
        (gathered[:, :: size_x - 1, :: size_y - 1], own_part)
    )
    got += [
        cross(corners_from[:, 1:, 1:], corners_from[:, :1, :1], "space", CY + 1),
        cross(corners_from[:, 1:, :1], corners_from[:, :1, 1:], "space", CY - 1),
    ]
    parity = lax.axis_index("chan") % 2
    on_first = parity == 0
    width = lax.axis_size("chan")
    pairs_core = [(lane, lane ^ 1) for lane in range(width)]
    mine_face = conv(
        got[0], lax.dynamic_slice_in_dim(weight, 2 * parity, 1, axis=0), ((0, 0), (1, 1), (1, 1))
    )
    sizes = [piece[0].size for piece in got]
    early = jnp.concatenate([piece.reshape(width_in, -1) for piece in got[:2]], axis=1)
    early_other = lax.ppermute(early, "chan", pairs_core)
    face_other = early_other[:, : sizes[0]].reshape(got[0].shape)
    row_other = early_other[:, sizes[0] :].reshape(got[1].shape)
    other_face = conv(
        face_other,
        lax.dynamic_slice_in_dim(weight, 2 - 2 * parity, 1, axis=0),
        ((0, 0), (1, 1), (1, 1)),
    )
    corners_got, own_part, mine_face, other_face, row_other = lax.optimization_barrier(
        (got[2:], own_part, mine_face, other_face, row_other)
    )
    late = jnp.concatenate([piece.reshape(width_in, -1) for piece in corners_got], axis=1)
    late_other = lax.ppermute(late, "chan", pairs_core)
    corner_a_other = late_other[:, : sizes[2]].reshape(got[2].shape)
    corner_b_other = late_other[:, sizes[2] :].reshape(got[3].shape)
    lower_row = jnp.where(on_first, got[1], row_other)
    upper_row = jnp.where(on_first, row_other, got[1])
    corner_ll = jnp.where(on_first, corners_got[0], corner_a_other)
    corner_hh = jnp.where(on_first, corner_a_other, corners_got[0])
    corner_lh = jnp.where(on_first, corners_got[1], corner_b_other)
    corner_hl = jnp.where(on_first, corner_b_other, corners_got[1])
    face_part = jnp.where(
        on_first,
        jnp.concatenate([mine_face, other_face], axis=0),
        jnp.concatenate([other_face, mine_face], axis=0),
    )
    place_y = (lax.axis_index("space") + 4) % 8
    lower_rim = jnp.concatenate([corner_ll, lower_row, corner_hl], axis=1)
    upper_rim = jnp.concatenate([corner_lh, upper_row, corner_hh], axis=1)
    lower_rim = jnp.where(place_y > 0, lower_rim, jnp.zeros_like(lower_rim))
    upper_rim = jnp.where(place_y < 7, upper_rim, jnp.zeros_like(upper_rim))
    lower_part = conv(lower_rim, weight[:, :1], ((0, 0), (0, 0), (1, 1)))
    upper_part = conv(upper_rim, weight[:, 2:], ((0, 0), (0, 0), (1, 1)))
    width_out = own_part.shape[1]
    middle = jnp.zeros((size_x, width_out, size_y - 2, size_z), jnp.float32)
    rim_part = jnp.concatenate([lower_part, middle, upper_part], axis=2)
    before = own_part + face_part + rim_part + conv_bias[None, :, None, None]
    result = jnp.maximum(before, negative_slope * before)
    return result.reshape(1, size_x, width_out, size_y * size_z)


def solution(mesh):
    placed = (P("space", None, "chan", None), P(None, None, None, "chan", None), P("chan"))
    return jax.shard_map(
        body, mesh=mesh, in_specs=placed, out_specs=P("space", None, "chan", None), check_vma=False
    )
```

profile of v0, /device:TPU:1, one launch (start us, length us, event | category | flops | bytes accessed | tf_op | source)
XLA Modules:
  0.0 60.7 jit_solution(9849114820241428272)
XLA Ops:
  0.0 0.9 %convert_element_type.8 = bf16[1,2,64,256]{3,2,1,0:T(8,128)(2,1)S(1)} convert(f32[1,2,64,256]{3,2,1,0:T(8,128)} %param.3) | non-fusion elementwise | flops 32768 | bytes 196608 | tf_op jit(solution)/shard_map/convert_element_type | solution.py:49
  0.9 0.1 copy.89
  1.0 21.7 %all_gather.3 = bf16[512,2,256]{2,1,0:T(2,128)(2,1)S(1)} all-gather(bf16[64,2,256]{2,1,0:T(2,128)(2,1)S(1)} %bitcast.122), channel_id=1, replica_groups=mesh['space'=64,'chan'=8] {'chan'}, dimensions={0}, use_global_device_ids=true | all-gather | bytes 589824 | tf_op jit(solution)/shard_map/all_gather | solution.py:50
  22.7 0.7 %copy.46 = bf16[512,2,256]{0,2,1:T(8,128)(2,1)S(1)} copy(bf16[512,2,256]{2,1,0:T(2,128)(2,1)S(1)} %all_gather.3) | data formatting | bytes 1048576 | tf_op jit(solution)/shard_map/all_gather | solution.py:50
  23.5 10.9 %collective-permute-start.3 = (bf16[512,2,1,32]{0,3,2,1:T(8,128)(2,1)S(1)}, bf16[512,2,1,32]{0,3,2,1:T(8,128)(2,1)S(1)}, u32[]{:S(2)}, u32[]{:S(2)}) collective-permute-start(bf16[512,2,1,32]{0,3,2,1:T(8,128)(2,1)S(1)} %slice_select_fusion.1), channel_id=1, source_target_pairs={{0,8},{1,509},{2,10},{3,511},{4,12},{5,505},{6,14},{7,507},{8,16},... | collective-permute-start | bytes 196616 | tf_op jit(solution)/shard_map/ppermute | solution.py:24
  34.4 1.9 %collective-permute-start.2 = (bf16[512,1,8,32]{0,3,2,1:T(8,128)(2,1)S(1)}, bf16[512,1,8,32]{0,3,2,1:T(8,128)(2,1)S(1)}, u32[]{:S(2)}, u32[]{:S(2)}) collective-permute-start(bf16[512,1,8,32]{0,3,2,1:T(8,128)(2,1)S(1)} %slice_select_fusion), channel_id=1, source_target_pairs={{0,68},{1,453},{2,70},{3,455},{4,64},{5,449},{6,66},{7,451},{8,76}... | collective-permute-start | bytes 786440 | tf_op jit(solution)/shard_map/ppermute | solution.py:24
  36.3 0.3 copy.82
  36.7 0.2 copy.50
  36.9 0.1 slice.70
  37.0 1.1 %copy-done.1 = bf16[3,3,3,64,512]{4,3,2,1,0:T(8,128)(2,1)S(1)} copy-done((bf16[3,3,3,64,512]{4,3,2,1,0:T(8,128)(2,1)S(1)}, bf16[3,3,3,64,512]{4,3,2,1,0:T(8,128)(2,1)}, u32[]{:S(2)}) %copy-start.1) | copy-done | bytes 1769496
  38.1 4.7 %convolution_select_fusion = f32[2,8,8,5,64]{4,2,3,1,0:T(8,128)S(1)} fusion(bf16[3,3,3,64,512]{4,3,2,1,0:T(8,128)(2,1)S(1)} %copy-done.1, bf16[512,2,8,1,7,2]{0,4,5,2,1,3:T(8,128)(2,1)S(1)} %slice.70, bf16[512,2,8,1,8,5]{0,4,5,2,1,3:T(8,128)(2,1)S(1)} %copy.50, pred[8,5]{0,1:T(8,128)(4,1)S(1)} %copy-done.2), kind=kOutput, calls=%fused_computation.2 | convolution fusion | flops 694853632 | bytes 2818088 | tf_op jit(solution)/shard_map/conv_general_dilated | solution.py:35
  42.8 0.1 copy.51
  43.0 1.9 %collective-permute-start.1 = (bf16[512,1,1,32]{0,3,2,1:T(8,128)(2,1)S(1)}, bf16[512,1,1,32]{0,3,2,1:T(8,128)(2,1)S(1)}, u32[]{:S(2)}, u32[]{:S(2)}) collective-permute-start(bf16[512,1,1,32]{0,3,2,1:T(8,128)(2,1)S(1)} %get-tuple-element.23), channel_id=1, source_target_pairs={{0,56},{1,461},{2,58},{3,463},{4,60},{5,457},{6,62},{7,459},{8,68}... | collective-permute-start | bytes 98312 | tf_op jit(solution)/shard_map/ppermute | solution.py:24
  44.9 4.8 %collective-permute-start = (bf16[512,1,1,32]{0,3,2,1:T(8,128)(2,1)S(1)}, bf16[512,1,1,32]{0,3,2,1:T(8,128)(2,1)S(1)}, u32[]{:S(2)}, u32[]{:S(2)}) collective-permute-start(bf16[512,1,1,32]{0,3,2,1:T(8,128)(2,1)S(1)} %get-tuple-element.24), channel_id=1, source_target_pairs={{0,76},{1,441},{2,78},{3,443},{4,72},{5,445},{6,74},{7,447},{8,84}... | collective-permute-start | bytes 98312 | tf_op jit(solution)/shard_map/ppermute | solution.py:24
  49.8 0.1 pad.11.clone
  49.9 0.1 copy.83
  50.0 0.1 copy.54
  50.2 1.9 %collective-permute-start.4 = (bf16[512,320]{0,1:T(8,128)(2,1)S(1)}, bf16[512,320]{0,1:T(8,128)(2,1)S(1)}, u32[]{:S(2)}, u32[]{:S(2)}) collective-permute-start(bf16[512,320]{0,1:T(8,128)(2,1)S(1)} %pad_maximum_fusion), channel_id=1, source_target_pairs={{0,1},{1,0},{2,3},{3,2},{4,5},{5,4},{6,7},{7,6},{8,9},{9,8},{10,11... | collective-permute-start | bytes 983048 | tf_op jit(solution)/shard_map/ppermute | solution.py:74
  52.2 0.9 %convolution_select_fusion.2 = f32[1,8,8,5,64]{4,2,3,1,0:T(8,128)S(1)} fusion(bf16[3,3,3,64,512]{4,3,2,1,0:T(8,128)(2,1)S(1)} %copy-done.1, s32[]{:T(128)S(6)} %select_n.123, bf16[512,1,8,1,7,2]{0,4,5,2,3,1:T(8,128)(2,1)S(1)} %slice.74, bf16[512,1,8,1,8,5]{0,4,5,2,3,1:T(8,128)(2,1)S(1)} %copy.54, pred[8,5]{0,1:T(8,128)(4,1)S(1)} %copy-done.2), kind=kOutput, calls=%fused_computation.4 | convolution fusion | flops 174411776 | bytes 1131524 | tf_op jit(solution)/shard_map/conv_general_dilated | solution.py:35
  53.1 0.6 %collective-permute-done.4 = bf16[512,320]{0,1:T(8,128)(2,1)S(1)} collective-permute-done((bf16[512,320]{0,1:T(8,128)(2,1)S(1)}, bf16[512,320]{0,1:T(8,128)(2,1)S(1)}, u32[]{:S(2)}, u32[]{:S(2)}) %collective-permute-start.4) | collective-permute-done | bytes 327712 | tf_op jit(solution)/shard_map/ppermute | solution.py:74
  53.8 0.2 copy.84
  54.0 0.1 copy.59
  54.1 0.9 %convolution_select_fusion.1 = f32[1,8,8,5,64]{4,2,3,1,0:T(8,128)S(1)} fusion(bf16[3,3,3,64,512]{4,3,2,1,0:T(8,128)(2,1)S(1)} %copy-done.1, s32[]{:T(128)S(6)} %select_n.126, bf16[512,1,8,1,7,2]{0,4,5,2,3,1:T(8,128)(2,1)S(1)} %slice.79, bf16[512,1,8,1,8,5]{0,4,5,2,3,1:T(8,128)(2,1)S(1)} %copy.59, pred[8,5]{0,1:T(8,128)(4,1)S(1)} %copy-done.2), kind=kOutput, calls=%fused_computation.3 | convolution fusion | flops 174411776 | bytes 1131524 | tf_op jit(solution)/shard_map/conv_general_dilated | solution.py:35
  55.2 2.1 %collective-permute-start.5 = (bf16[512,64]{0,1:T(8,128)(2,1)S(1)}, bf16[512,64]{0,1:T(8,128)(2,1)S(1)}, u32[]{:S(2)}, u32[]{:S(2)}) collective-permute-start(bf16[512,64]{0,1:T(8,128)(2,1)S(1)} %pad_maximum_fusion.1), channel_id=1, source_target_pairs={{0,1},{1,0},{2,3},{3,2},{4,5},{5,4},{6,7},{7,6},{8,9},{9,8},{10,11... | collective-permute-start | bytes 196616 | tf_op jit(solution)/shard_map/ppermute | solution.py:86
  57.2 1.1 %collective-permute-done.5 = bf16[512,64]{0,1:T(8,128)(2,1)S(1)} collective-permute-done((bf16[512,64]{0,1:T(8,128)(2,1)S(1)}, bf16[512,64]{0,1:T(8,128)(2,1)S(1)}, u32[]{:S(2)}, u32[]{:S(2)}) %collective-permute-start.5) | collective-permute-done | bytes 65568 | tf_op jit(solution)/shard_map/ppermute | solution.py:86
  58.4 0.1 copy.85
  58.6 0.3 convolution_select_fusion.4
  59.0 0.1 copy.86
  59.1 0.1 pad.8.clone
  59.3 0.3 convolution_select_fusion.3
  59.7 0.2 multiply_maximum_fusion
  59.9 0.8 %copy.79 = f32[1,2,64,256]{3,2,1,0:T(8,128)} copy(f32[1,2,64,256]{2,3,1,0:T(8,128)S(1)} %bitcast.116) | data formatting | bytes 262144 | tf_op jit(solution)/shard_map/reshape | solution.py:112
  (43 shorter events, 0.8 us)
Async XLA Ops:
  23.5 26.7 %collective-permute-start.3 = (bf16[512,2,1,32]{0,3,2,1:T(8,128)(2,1)S(1)}, bf16[512,2,1,32]{0,3,2,1:T(8,128)(2,1)S(1)}, u32[]{:S(2)}, u32[]{:S(2)}) collective-permute-start(bf16[512,2,1,32]{0,3,2,1:T(8,128)(2,1)S(1)} %slice_select_fusion.1), channel_id=1, source_target_pairs={{0,8},{1,509},{2,10},{3,511},{4,12},{5,505},{6,14},{7,507},{8,16},... | collective-permute-start | bytes 196616 | tf_op jit(solution)/shard_map/ppermute | solution.py:24
  34.4 15.4 %collective-permute-start.2 = (bf16[512,1,8,32]{0,3,2,1:T(8,128)(2,1)S(1)}, bf16[512,1,8,32]{0,3,2,1:T(8,128)(2,1)S(1)}, u32[]{:S(2)}, u32[]{:S(2)}) collective-permute-start(bf16[512,1,8,32]{0,3,2,1:T(8,128)(2,1)S(1)} %slice_select_fusion), channel_id=1, source_target_pairs={{0,68},{1,453},{2,70},{3,455},{4,64},{5,449},{6,66},{7,451},{8,76}... | collective-permute-start | bytes 786440 | tf_op jit(solution)/shard_map/ppermute | solution.py:24
  36.6 1.5 %copy-start.1 = (bf16[3,3,3,64,512]{4,3,2,1,0:T(8,128)(2,1)S(1)}, bf16[3,3,3,64,512]{4,3,2,1,0:T(8,128)(2,1)}, u32[]{:S(2)}) copy-start(bf16[3,3,3,64,512]{4,3,2,1,0:T(8,128)(2,1)} %param.4) | copy-start | bytes 5308420
  36.7 1.5 %copy-start.2 = (pred[8,5]{0,1:T(8,128)(4,1)S(1)}, pred[8,5]{0,1:T(8,128)(4,1)}, u32[]{:S(2)}) copy-start(pred[8,5]{0,1:T(8,128)(4,1)} %constant.75) | copy-start | bytes 124
  43.0 12.2 %collective-permute-start.1 = (bf16[512,1,1,32]{0,3,2,1:T(8,128)(2,1)S(1)}, bf16[512,1,1,32]{0,3,2,1:T(8,128)(2,1)S(1)}, u32[]{:S(2)}, u32[]{:S(2)}) collective-permute-start(bf16[512,1,1,32]{0,3,2,1:T(8,128)(2,1)S(1)} %get-tuple-element.23), channel_id=1, source_target_pairs={{0,56},{1,461},{2,58},{3,463},{4,60},{5,457},{6,62},{7,459},{8,68}... | collective-permute-start | bytes 98312 | tf_op jit(solution)/shard_map/ppermute | solution.py:24
  44.9 10.2 %collective-permute-start = (bf16[512,1,1,32]{0,3,2,1:T(8,128)(2,1)S(1)}, bf16[512,1,1,32]{0,3,2,1:T(8,128)(2,1)S(1)}, u32[]{:S(2)}, u32[]{:S(2)}) collective-permute-start(bf16[512,1,1,32]{0,3,2,1:T(8,128)(2,1)S(1)} %get-tuple-element.24), channel_id=1, source_target_pairs={{0,76},{1,441},{2,78},{3,443},{4,72},{5,445},{6,74},{7,447},{8,84}... | collective-permute-start | bytes 98312 | tf_op jit(solution)/shard_map/ppermute | solution.py:24
  50.2 3.5 %collective-permute-start.4 = (bf16[512,320]{0,1:T(8,128)(2,1)S(1)}, bf16[512,320]{0,1:T(8,128)(2,1)S(1)}, u32[]{:S(2)}, u32[]{:S(2)}) collective-permute-start(bf16[512,320]{0,1:T(8,128)(2,1)S(1)} %pad_maximum_fusion), channel_id=1, source_target_pairs={{0,1},{1,0},{2,3},{3,2},{4,5},{5,4},{6,7},{7,6},{8,9},{9,8},{10,11... | collective-permute-start | bytes 983048 | tf_op jit(solution)/shard_map/ppermute | solution.py:74
  55.2 3.1 %collective-permute-start.5 = (bf16[512,64]{0,1:T(8,128)(2,1)S(1)}, bf16[512,64]{0,1:T(8,128)(2,1)S(1)}, u32[]{:S(2)}, u32[]{:S(2)}) collective-permute-start(bf16[512,64]{0,1:T(8,128)(2,1)S(1)} %pad_maximum_fusion.1), channel_id=1, source_target_pairs={{0,1},{1,0},{2,3},{3,2},{4,5},{5,4},{6,7},{7,6},{8,9},{9,8},{10,11... | collective-permute-start | bytes 196616 | tf_op jit(solution)/shard_map/ppermute | solution.py:86
  59.0 0.7 %copy-start = (f32[64]{0:T(128)S(1)}, f32[64]{0:T(128)}, u32[]{:S(2)}) copy-start(f32[64]{0:T(128)} %param.5) | copy-start | bytes 772
where the time goes:
time: 61 us; the launch traced here: 60.7 us
  starting transfers between devices  23.5 us (39%)
  blocking collectives  21.7 us (36%)
  matrix products  7.21 us (12%)
  local copies, waits for them, and re-layouts  4.76 us (8%)
  waiting for transfers between devices  1.69 us (3%)
  other arithmetic  1.23 us (2%)
    all_gather x1, blocking collectives, body(): gathered = lax.all_gather(own_block, 'chan', axis=0, tiled=True)  21.7 us
    ppermute x4, starting transfers between devices, cross(): return lax.ppermute(sent, (axis, 'chan'), pairs)  19.6 us
    conv_general_dilated x5, matrix products, conv(): lax.conv_general_dilated(field[None], taps, window_strides=(1, 1, 1), pad...  7.21 us
    ppermute x1, starting transfers between devices, body(): late_other = lax.ppermute(late, 'chan', pairs_core)  2.06 us
    unnamed x14, local copies, waits for them, and re-layouts  2.03 us
    ppermute x1, starting transfers between devices, body(): early_other = lax.ppermute(early, 'chan', pairs_core)  1.92 us
  transfers between devices with their start and end apart: 6, of which 2 were waited for; matrix products, arithmetic and copies ran while one was open for 13% of the time, Pallas kernels for 0%

commit v1 on v0

--- a/solution.py
+++ b/solution.py
@@ -2,6 +2,7 @@
 import jax.numpy as jnp
 from jax import lax
 from jax.sharding import PartitionSpec as P
+from jax.lax import all_to_all, axis_size
 
 CY = 8
 negative_slope = 0.3
@@ -47,7 +48,10 @@
     size_y = CY
     size_z = activation.shape[3] // size_y
     own_block = activation[0].astype(jnp.bfloat16).transpose(1, 0, 2)
-    gathered = lax.all_gather(own_block, "chan", axis=0, tiled=True)
+    cards = []
+    for _ in range(axis_size("chan")):
+        cards.append(own_block)
+    gathered = jnp.concatenate(all_to_all(jnp.stack(cards, axis=0), "chan", 0, 0), axis=0)
     gathered = gathered.reshape(-1, size_x, size_y, size_z)
     own_part = conv(gathered, weight, ((1, 1), (1, 1), (1, 1)))
     width_in = gathered.shape[0]

time: 61 us -> 67.4 us (1.10)
  the two profiles are of different devices: /device:TPU:1 before, /device:TPU:9 now
where the time goes in v1:
time: 67.4 us; the launch traced here: 67 us
  starting transfers between devices  36 us (53%)
  waiting for transfers between devices  16.6 us (25%)
  matrix products  7.26 us (11%)
  local copies, waits for them, and re-layouts  5.46 us (8%)
  other arithmetic  1.22 us (2%)
    ppermute x4, starting transfers between devices, cross(): return lax.ppermute(sent, (axis, 'chan'), pairs)  22.5 us
    all_to_all x1, waiting for transfers between devices, body(): all_to_all(jnp.stack(cards, axis=0), 'chan', 0, 0)  11.7 us
    all_to_all x1, starting transfers between devices, body(): all_to_all(jnp.stack(cards, axis=0), 'chan', 0, 0)  9.54 us
    conv_general_dilated x5, matrix products, conv(): lax.conv_general_dilated(field[None], taps, window_strides=(1, 1, 1), pad...  7.26 us
    ppermute x4, waiting for transfers between devices, cross(): return lax.ppermute(sent, (axis, 'chan'), pairs)  3.23 us
    ppermute x1, starting transfers between devices, body(): late_other = lax.ppermute(late, 'chan', pairs_core)  2.04 us
    ppermute x1, starting transfers between devices, body(): early_other = lax.ppermute(early, 'chan', pairs_core)  1.92 us
  transfers between devices with their start and end apart: 7, of which 4 were waited for; matrix products, arithmetic and copies ran while one was open for 12% of the time, Pallas kernels for 0%

profile of v1, /device:TPU:9, one launch (start us, length us, event | category | flops | bytes accessed | tf_op | source)
XLA Modules:
  0.0 67.0 jit_solution(18172971912420338242)
XLA Ops:
  0.0 0.9 %convert_bitcast_fusion = bf16[64,2,256]{2,0,1:T(8,128)(2,1)S(1)} fusion(f32[1,2,64,256]{3,2,1,0:T(8,128)} %param.3), kind=kLoop, calls=%fused_computation.67 | loop fusion | flops 32768 | bytes 196608 | tf_op jit(solution)/shard_map/transpose | solution.py:50
  0.9 0.8 %stack.2 = bf16[8,64,2,256]{3,1,2,0:T(8,128)(2,1)} broadcast(bf16[64,2,256]{2,0,1:T(8,128)(2,1)S(1)} %convert_bitcast_fusion), dimensions={1,2,3} | broadcast | bytes 589824 | tf_op jit(solution)/shard_map/stack | solution.py:54
  1.8 9.5 %all-to-all-start = ((bf16[8,64,2,256]{3,1,2,0:T(8,128)(2,1)}), bf16[8,64,2,256]{3,1,2,0:T(8,128)(2,1)S(1)}, u32[]{:S(2)}, u32[]{:S(2)}) async-start(bf16[8,64,2,256]{3,1,2,0:T(8,128)(2,1)} %stack.2), calls=%async_computation | async-start | bytes 1048576 | tf_op jit(solution)/shard_map/all_to_all | solution.py:54
  11.3 0.1 pad.11.clone
  11.4 11.7 %all-to-all-done = bf16[8,64,2,256]{3,1,2,0:T(8,128)(2,1)S(1)} async-done(((bf16[8,64,2,256]{3,1,2,0:T(8,128)(2,1)}), bf16[8,64,2,256]{3,1,2,0:T(8,128)(2,1)S(1)}, u32[]{:S(2)}, u32[]{:S(2)}) %all-to-all-start) | async-done | bytes 524320 | tf_op jit(solution)/shard_map/all_to_all | solution.py:54
  23.1 0.6 copy.52
  23.7 0.6 reshape_reshape.3
  24.3 0.6 reshape.181
  25.0 0.3 copy.89
  25.3 13.8 %collective-permute-start.3 = (bf16[512,2,1,32]{0,3,2,1:T(8,128)(2,1)S(1)}, bf16[512,2,1,32]{0,3,2,1:T(8,128)(2,1)S(1)}, u32[]{:S(2)}, u32[]{:S(2)}) collective-permute-start(bf16[512,2,1,32]{0,3,2,1:T(8,128)(2,1)S(1)} %bitcast_select_fusion.1), channel_id=1, source_target_pairs={{0,8},{1,509},{2,10},{3,511},{4,12},{5,505},{6,14},{7,507},{8,16},... | collective-permute-start | bytes 196616 | tf_op jit(solution)/shard_map/ppermute | solution.py:25
  39.2 0.2 copy.56
  39.4 4.7 %convolution_select_fusion = f32[2,8,8,5,64]{4,2,3,1,0:T(8,128)S(1)} fusion(bf16[3,3,3,64,512]{4,3,2,1,0:T(8,128)(2,1)S(1)} %copy-done.1, bf16[512,2,8,1,7,2]{0,4,5,2,1,3:T(8,128)(2,1)S(1)} %slice.70, bf16[512,2,8,1,8,5]{0,4,5,2,1,3:T(8,128)(2,1)S(1)} %copy.56, pred[8,5]{0,1:T(8,128)(4,1)S(1)} %copy-done.2), kind=kOutput, calls=%fused_computation.2 | convolution fusion | flops 694853632 | bytes 2818088 | tf_op jit(solution)/shard_map/conv_general_dilated | solution.py:36
  44.2 1.9 %collective-permute-start.2 = (bf16[512,1,8,32]{0,3,2,1:T(8,128)(2,1)S(1)}, bf16[512,1,8,32]{0,3,2,1:T(8,128)(2,1)S(1)}, u32[]{:S(2)}, u32[]{:S(2)}) collective-permute-start(bf16[512,1,8,32]{0,3,2,1:T(8,128)(2,1)S(1)} %slice_select_fusion), channel_id=1, source_target_pairs={{0,68},{1,453},{2,70},{3,455},{4,64},{5,449},{6,66},{7,451},{8,76}... | collective-permute-start | bytes 786440 | tf_op jit(solution)/shard_map/ppermute | solution.py:25
  46.2 1.9 %collective-permute-start.1 = (bf16[512,1,1,32]{0,3,2,1:T(8,128)(2,1)S(1)}, bf16[512,1,1,32]{0,3,2,1:T(8,128)(2,1)S(1)}, u32[]{:S(2)}, u32[]{:S(2)}) collective-permute-start(bf16[512,1,1,32]{0,3,2,1:T(8,128)(2,1)S(1)} %get-tuple-element.21), channel_id=1, source_target_pairs={{0,56},{1,461},{2,58},{3,463},{4,60},{5,457},{6,62},{7,459},{8,68}... | collective-permute-start | bytes 98312 | tf_op jit(solution)/shard_map/ppermute | solution.py:25
  48.1 4.8 %collective-permute-start = (bf16[512,1,1,32]{0,3,2,1:T(8,128)(2,1)S(1)}, bf16[512,1,1,32]{0,3,2,1:T(8,128)(2,1)S(1)}, u32[]{:S(2)}, u32[]{:S(2)}) collective-permute-start(bf16[512,1,1,32]{0,3,2,1:T(8,128)(2,1)S(1)} %get-tuple-element.22), channel_id=1, source_target_pairs={{0,76},{1,441},{2,78},{3,443},{4,72},{5,445},{6,74},{7,447},{8,84}... | collective-permute-start | bytes 98312 | tf_op jit(solution)/shard_map/ppermute | solution.py:25
  53.0 3.2 %collective-permute-done.2 = bf16[512,1,8,32]{0,3,2,1:T(8,128)(2,1)S(1)} collective-permute-done((bf16[512,1,8,32]{0,3,2,1:T(8,128)(2,1)S(1)}, bf16[512,1,8,32]{0,3,2,1:T(8,128)(2,1)S(1)}, u32[]{:S(2)}, u32[]{:S(2)}) %collective-permute-start.2) | collective-permute-done | bytes 262176 | tf_op jit(solution)/shard_map/ppermute | solution.py:25
  56.2 0.1 copy.90
  56.4 0.1 copy.60
  56.6 1.9 %collective-permute-start.4 = (bf16[512,320]{0,1:T(8,128)(2,1)S(1)}, bf16[512,320]{0,1:T(8,128)(2,1)S(1)}, u32[]{:S(2)}, u32[]{:S(2)}) collective-permute-start(bf16[512,320]{0,1:T(8,128)(2,1)S(1)} %pad_maximum_fusion), channel_id=1, source_target_pairs={{0,1},{1,0},{2,3},{3,2},{4,5},{5,4},{6,7},{7,6},{8,9},{9,8},{10,11... | collective-permute-start | bytes 983048 | tf_op jit(solution)/shard_map/ppermute | solution.py:78
  58.5 0.9 %convolution_select_fusion.2 = f32[1,8,8,5,64]{4,2,3,1,0:T(8,128)S(1)} fusion(bf16[3,3,3,64,512]{4,3,2,1,0:T(8,128)(2,1)S(1)} %copy-done.1, s32[]{:T(128)S(6)} %select_n.123, bf16[512,1,8,1,7,2]{0,4,5,2,3,1:T(8,128)(2,1)S(1)} %slice.74, bf16[512,1,8,1,8,5]{0,4,5,2,3,1:T(8,128)(2,1)S(1)} %copy.60, pred[8,5]{0,1:T(8,128)(4,1)S(1)} %copy-done.2), kind=kOutput, calls=%fused_computation.4 | convolution fusion | flops 174411776 | bytes 1131524 | tf_op jit(solution)/shard_map/conv_general_dilated | solution.py:36
  59.5 0.6 collective-permute-done.4
  60.1 0.2 copy.91
  60.3 0.1 copy.66
  60.5 0.9 %convolution_select_fusion.1 = f32[1,8,8,5,64]{4,2,3,1,0:T(8,128)S(1)} fusion(bf16[3,3,3,64,512]{4,3,2,1,0:T(8,128)(2,1)S(1)} %copy-done.1, s32[]{:T(128)S(6)} %select_n.126, bf16[512,1,8,1,7,2]{0,4,5,2,3,1:T(8,128)(2,1)S(1)} %slice.79, bf16[512,1,8,1,8,5]{0,4,5,2,3,1:T(8,128)(2,1)S(1)} %copy.66, pred[8,5]{0,1:T(8,128)(4,1)S(1)} %copy-done.2), kind=kOutput, calls=%fused_computation.3 | convolution fusion | flops 174411776 | bytes 1131524 | tf_op jit(solution)/shard_map/conv_general_dilated | solution.py:36
  61.5 2.0 %collective-permute-start.5 = (bf16[512,64]{0,1:T(8,128)(2,1)S(1)}, bf16[512,64]{0,1:T(8,128)(2,1)S(1)}, u32[]{:S(2)}, u32[]{:S(2)}) collective-permute-start(bf16[512,64]{0,1:T(8,128)(2,1)S(1)} %pad_maximum_fusion.1), channel_id=1, source_target_pairs={{0,1},{1,0},{2,3},{3,2},{4,5},{5,4},{6,7},{7,6},{8,9},{9,8},{10,11... | collective-permute-start | bytes 196616 | tf_op jit(solution)/shard_map/ppermute | solution.py:90
  63.6 1.1 %collective-permute-done.5 = bf16[512,64]{0,1:T(8,128)(2,1)S(1)} collective-permute-done((bf16[512,64]{0,1:T(8,128)(2,1)S(1)}, bf16[512,64]{0,1:T(8,128)(2,1)S(1)}, u32[]{:S(2)}, u32[]{:S(2)}) %collective-permute-start.5) | collective-permute-done | bytes 65568 | tf_op jit(solution)/shard_map/ppermute | solution.py:90
  64.7 0.1 copy.92
  65.0 0.3 convolution_select_fusion.4
  65.4 0.1 copy.93
  65.6 0.3 convolution_select_fusion.3
  66.1 0.1 multiply_maximum_fusion
  66.3 0.8 %copy.86 = f32[1,2,64,256]{3,2,1,0:T(8,128)} copy(f32[1,2,64,256]{2,3,1,0:T(8,128)S(1)} %bitcast.119) | data formatting | bytes 262144 | tf_op jit(solution)/shard_map/reshape | solution.py:116
  (47 shorter events, 0.9 us)
Async XLA Ops:
  1.8 21.3 %all-to-all-start = ((bf16[8,64,2,256]{3,1,2,0:T(8,128)(2,1)}), bf16[8,64,2,256]{3,1,2,0:T(8,128)(2,1)S(1)}, u32[]{:S(2)}, u32[]{:S(2)}) async-start(bf16[8,64,2,256]{3,1,2,0:T(8,128)(2,1)} %stack.2), calls=%async_computation | async-start | bytes 1048576 | tf_op jit(solution)/shard_map/all_to_all | solution.py:54
  25.3 14.2 %copy-start.1 = (bf16[3,3,3,64,512]{4,3,2,1,0:T(8,128)(2,1)S(1)}, bf16[3,3,3,64,512]{4,3,2,1,0:T(8,128)(2,1)}, u32[]{:S(2)}) copy-start(bf16[3,3,3,64,512]{4,3,2,1,0:T(8,128)(2,1)} %param.4) | copy-start | bytes 5308420
  25.3 14.2 %copy-start.2 = (pred[8,5]{0,1:T(8,128)(4,1)S(1)}, pred[8,5]{0,1:T(8,128)(4,1)}, u32[]{:S(2)}) copy-start(pred[8,5]{0,1:T(8,128)(4,1)} %constant.75) | copy-start | bytes 124
  25.3 31.2 %collective-permute-start.3 = (bf16[512,2,1,32]{0,3,2,1:T(8,128)(2,1)S(1)}, bf16[512,2,1,32]{0,3,2,1:T(8,128)(2,1)S(1)}, u32[]{:S(2)}, u32[]{:S(2)}) collective-permute-start(bf16[512,2,1,32]{0,3,2,1:T(8,128)(2,1)S(1)} %bitcast_select_fusion.1), channel_id=1, source_target_pairs={{0,8},{1,509},{2,10},{3,511},{4,12},{5,505},{6,14},{7,507},{8,16},... | collective-permute-start | bytes 196616 | tf_op jit(solution)/shard_map/ppermute | solution.py:25
  44.2 12.0 %collective-permute-start.2 = (bf16[512,1,8,32]{0,3,2,1:T(8,128)(2,1)S(1)}, bf16[512,1,8,32]{0,3,2,1:T(8,128)(2,1)S(1)}, u32[]{:S(2)}, u32[]{:S(2)}) collective-permute-start(bf16[512,1,8,32]{0,3,2,1:T(8,128)(2,1)S(1)} %slice_select_fusion), channel_id=1, source_target_pairs={{0,68},{1,453},{2,70},{3,455},{4,64},{5,449},{6,66},{7,451},{8,76}... | collective-permute-start | bytes 786440 | tf_op jit(solution)/shard_map/ppermute | solution.py:25
  46.2 15.3 %collective-permute-start.1 = (bf16[512,1,1,32]{0,3,2,1:T(8,128)(2,1)S(1)}, bf16[512,1,1,32]{0,3,2,1:T(8,128)(2,1)S(1)}, u32[]{:S(2)}, u32[]{:S(2)}) collective-permute-start(bf16[512,1,1,32]{0,3,2,1:T(8,128)(2,1)S(1)} %get-tuple-element.21), channel_id=1, source_target_pairs={{0,56},{1,461},{2,58},{3,463},{4,60},{5,457},{6,62},{7,459},{8,68}... | collective-permute-start | bytes 98312 | tf_op jit(solution)/shard_map/ppermute | solution.py:25
  48.1 13.3 %collective-permute-start = (bf16[512,1,1,32]{0,3,2,1:T(8,128)(2,1)S(1)}, bf16[512,1,1,32]{0,3,2,1:T(8,128)(2,1)S(1)}, u32[]{:S(2)}, u32[]{:S(2)}) collective-permute-start(bf16[512,1,1,32]{0,3,2,1:T(8,128)(2,1)S(1)} %get-tuple-element.22), channel_id=1, source_target_pairs={{0,76},{1,441},{2,78},{3,443},{4,72},{5,445},{6,74},{7,447},{8,84}... | collective-permute-start | bytes 98312 | tf_op jit(solution)/shard_map/ppermute | solution.py:25
  56.6 3.5 %collective-permute-start.4 = (bf16[512,320]{0,1:T(8,128)(2,1)S(1)}, bf16[512,320]{0,1:T(8,128)(2,1)S(1)}, u32[]{:S(2)}, u32[]{:S(2)}) collective-permute-start(bf16[512,320]{0,1:T(8,128)(2,1)S(1)} %pad_maximum_fusion), channel_id=1, source_target_pairs={{0,1},{1,0},{2,3},{3,2},{4,5},{5,4},{6,7},{7,6},{8,9},{9,8},{10,11... | collective-permute-start | bytes 983048 | tf_op jit(solution)/shard_map/ppermute | solution.py:78
  61.5 3.1 %collective-permute-start.5 = (bf16[512,64]{0,1:T(8,128)(2,1)S(1)}, bf16[512,64]{0,1:T(8,128)(2,1)S(1)}, u32[]{:S(2)}, u32[]{:S(2)}) collective-permute-start(bf16[512,64]{0,1:T(8,128)(2,1)S(1)} %pad_maximum_fusion.1), channel_id=1, source_target_pairs={{0,1},{1,0},{2,3},{3,2},{4,5},{5,4},{6,7},{7,6},{8,9},{9,8},{10,11... | collective-permute-start | bytes 196616 | tf_op jit(solution)/shard_map/ppermute | solution.py:90
  65.3 0.7 %copy-start = (f32[64]{0:T(128)S(1)}, f32[64]{0:T(128)}, u32[]{:S(2)}) copy-start(f32[64]{0:T(128)} %param.5) | copy-start | bytes 772
